TPU v7x, 512 devices: a whole 4x4x16 slice. The times are simulated.
512 devices in a mesh: sub: 128 (over y, z, core), case: 4 (over x).
Axes of the slice: x: 4, y: 4, z: 16, core: 2. Of those that a mesh axis runs over, the one named last changes fastest.
Arguments:
- load_interior: float32 [128, 128, 4096], P('sub', None, 'case'), may hold values from -6 to 6
- load_boundary: float32 [128, 128, 1024], P('sub', None, 'case'), may hold values from -6 to 6
- cond_blocks: float32 [128, 128, 4096], P('sub', 'case'), may hold values from -0.25 to 0.25
- block_rows: int32 [128, 128], P('sub', 'case'), may hold values from 0 to 15
- block_cols: int32 [128, 128], P('sub', 'case'), may hold values from 0 to 63, as said below
- interface_maps: int32 [128, 7, 2, 1024], P('sub'), may hold values from 0 to 1023, as said below
- merge_maps: float32 [128, 7, 1024, 512], P('sub', None, 'case'), as said below
Outputs:
- leaf_loads: float32 [128, 1024, 128], P('sub', 'case')
- node_loads: float32 [128, 1024, 128], P('sub', 'case')
Inputs may be any that keep to these rules, and one draw needn't show every extreme that they name: `block_cols`: entry k of a substructure's row lies in [(k // 32) * 16, (k // 32 + 1) * 16); blocks may repeat. `interface_maps`: each row of 1024 entries is a permutation; at level index l, slots that agree in all but their lowest l + 1 bits hold equal entries. `merge_maps`: at level index l, slots that agree in all but their lowest l + 1 bits hold equal entries.
All inputs are finite; a program needn't handle non-finite values.
Results may differ from a plain program's by a relative error of at most 0.0003.
Values sent between devices are 32-bit elements; how exact they have to be, the bound alone decides.
No kernel may reach another device: no remote copies, remote signals or barrier semaphores. Data moves between devices by JAX's collectives and lax.ppermute only.
A program may use at most 64 MiB of HBM per device.

v0:
```python
import jax
import jax.numpy as jnp
from jax import lax
from jax.sharding import PartitionSpec as P

BLK = 64


def from_partner(value, axis, distance):
    mask = 2**distance
    pairs = [(source, source ^ mask) for source in range(lax.axis_size(axis))]
    return lax.ppermute(value, axis, pairs)


def on_device(
    load_interior, load_boundary, cond_blocks, block_rows, block_cols, interface_maps, merge_maps
):
    interior, boundary = (
        lax.all_to_all(load_interior, "sub", split_axis=1, concat_axis=0, tiled=True),
        lax.all_to_all(load_boundary, "sub", split_axis=1, concat_axis=0, tiled=True),
    )
    interior = jnp.transpose(interior[:, 0, :])
    boundary = jnp.transpose(boundary[:, 0, :])
    local_rows = interior.shape[0]
    num_cases = interior.shape[1]
    block_count = cond_blocks.shape[1]
    block_size = BLK
    blocks = cond_blocks[0].reshape(block_count, block_size, block_size)
    quarter = boundary.shape[0]
    groups = lax.axis_size("case")
    full_rows = quarter * groups
    position = lax.axis_index("case")
    local_cols = block_cols[0] - position * (local_rows // block_size)
    pieces = jnp.take(
        interior.reshape(local_rows // block_size, block_size, num_cases), local_cols, axis=0
    )
    products = jnp.einsum("krc,kcn->krn", blocks, pieces, precision=lax.Precision.HIGHEST)
    row_blocks = full_rows // block_size
    onehot = (block_rows[0][None, :] == jnp.arange(row_blocks, dtype=jnp.int32)[:, None]).astype(
        jnp.float32
    )
    partial_value = jnp.dot(
        onehot,
        products.reshape(block_count, block_size * num_cases),
        precision=lax.Precision.HIGHEST,
    )
    partial_value = partial_value.reshape(full_rows, num_cases)
    embedded = lax.dynamic_update_slice(
        jnp.zeros((full_rows, num_cases), jnp.float32), boundary, (position * quarter, 0)
    )
    contribution = embedded - partial_value
    current = lax.psum(contribution, "case")
    leaf_share = lax.dynamic_slice_in_dim(current, position * quarter, quarter, 0)
    slot = lax.axis_index("sub")
    levels = lax.axis_size("sub").bit_length() - 1
    nodes = jnp.zeros((quarter, num_cases), jnp.float32)
    for level in range(1, levels + 1):
        half = 1 << level - 1
        maps = interface_maps[0, level - 1]
        matrix = merge_maps[0, level - 1]
        shared_rows = matrix.shape[1]
        kept_index = jnp.concatenate([maps[0, shared_rows:], maps[1, shared_rows:] + full_rows])
        mine = lax.dynamic_slice_in_dim(kept_index, position * quarter, quarter)
        other = from_partner(current, "sub", level - 1)
        own_full, other_full = (current, other)
        upper = slot // half % 2 == 1
        left_full = jnp.where(upper, other_full, own_full)
        right_full = jnp.where(upper, own_full, other_full)
        stacked = jnp.concatenate([left_full, right_full], axis=0)
        shared = jnp.take(stacked, maps[0, :shared_rows], axis=0) + jnp.take(
            stacked, maps[1, :shared_rows] + full_rows, axis=0
        )
        parent = jnp.take(stacked, mine, axis=0) - jnp.dot(
            matrix, shared, precision=lax.Precision.HIGHEST
        )
        is_node = slot % (2 * half) == half
        if level == levels:
            is_node = jnp.logical_or(is_node, slot == 0)
        nodes = jnp.where(is_node, parent, nodes)
        if level < levels:
            current = lax.all_gather(parent, "case", axis=0, tiled=True)
    return (leaf_share[None], nodes[None])


def solution(mesh):
    placed = (
        P("sub", None, "case"),
        P("sub", None, "case"),
        P("sub", "case", None),
        P("sub", "case"),
        P("sub", "case"),
        P("sub", None, None, None),
        P("sub", None, "case", None),
    )
    return jax.shard_map(
        on_device,
        mesh=mesh,
        in_specs=placed,
        out_specs=(P("sub", "case", None), P("sub", "case", None)),
        check_vma=False,
    )
```

profile of v0, /device:TPU:8, one launch (start us, length us, event | category | flops | bytes accessed | tf_op | source)
XLA Modules:
  0.0 423.4 jit_solution(13161478264808261519)
XLA Ops:
  8.9 19.6 %all-to-all-start = ((f32[1,128,256]{2,0,1:T(1,128)}), f32[1,128,256]{2,0,1:T(1,128)S(1)}, u32[]{:S(2)}, u32[]{:S(2)}) async-start(f32[1,128,256]{2,0,1:T(1,128)} %copy.64), calls=%async_computation | async-start | bytes 262144 | tf_op jit(solution)/shard_map/all_to_all | solution.py:20
  28.5 2.4 copy.66
  32.8 12.9 %all-to-all-done = f32[1,128,256]{2,0,1:T(1,128)S(1)} async-done(((f32[1,128,256]{2,0,1:T(1,128)}), f32[1,128,256]{2,0,1:T(1,128)S(1)}, u32[]{:S(2)}, u32[]{:S(2)}) %all-to-all-start) | async-done | bytes 131104 | tf_op jit(solution)/shard_map/all_to_all | solution.py:20
  45.7 7.2 %all-to-all-start.1 = ((f32[1,128,1024]{2,0,1:T(1,128)}), f32[1,128,1024]{2,0,1:T(1,128)S(1)}, u32[]{:S(2)}, u32[]{:S(2)}) async-start(f32[1,128,1024]{2,0,1:T(1,128)} %copy.66), calls=%async_computation.1 | async-start | bytes 1048576 | tf_op jit(solution)/shard_map/all_to_all | solution.py:19
  55.1 31.4 %all-to-all-done.1 = f32[1,128,1024]{2,0,1:T(1,128)S(1)} async-done(((f32[1,128,1024]{2,0,1:T(1,128)}), f32[1,128,1024]{2,0,1:T(1,128)S(1)}, u32[]{:S(2)}, u32[]{:S(2)}) %all-to-all-start.1) | async-done | bytes 524320 | tf_op jit(solution)/shard_map/all_to_all | solution.py:19
  90.9 50.0 %all-reduce.2.cloned.1.call-done = f32[1024,128]{1,0:T(8,128)} async-done(((f32[1024,128]{1,0:T(8,128)}), f32[1024,128]{1,0:T(8,128)}) %all-reduce.2.cloned.1.call-update) | async-done | bytes 524304 | tf_op jit(solution)/shard_map/psum | solution.py:52
  150.9 12.8 %all_gather.18 = f32[1024,128]{0,1:T(8,128)S(1)} all-gather(f32[256,128]{0,1:T(8,128)S(1)} %fusion.8), channel_id=1, replica_groups=mesh['sub'=128,'case'=4] {'case'}, dimensions={0}, use_global_device_ids=true | all-gather | bytes 655360 | tf_op jit(solution)/shard_map/all_gather | solution.py:81
  163.6 3.6 collective-permute-start.1
  167.4 9.3 %collective-permute-done.1 = f32[1024,128]{0,1:T(8,128)S(1)} collective-permute-done((f32[1024,128]{0,1:T(8,128)S(1)}, f32[1024,128]{0,1:T(8,128)S(1)}, u32[]{:S(2)}, u32[]{:S(2)}) %collective-permute-start.1) | collective-permute-done | bytes 524320 | tf_op jit(solution)/shard_map/ppermute | solution.py:12
  182.0 13.1 %all_gather.19 = f32[1024,128]{0,1:T(8,128)S(1)} all-gather(f32[256,128]{0,1:T(8,128)S(1)} %fusion.7), channel_id=1, replica_groups=mesh['sub'=128,'case'=4] {'case'}, dimensions={0}, use_global_device_ids=true | all-gather | bytes 655360 | tf_op jit(solution)/shard_map/all_gather | solution.py:81
  195.1 4.4 %collective-permute-start.2 = (f32[1024,128]{0,1:T(8,128)S(1)}, f32[1024,128]{0,1:T(8,128)S(1)}, u32[]{:S(2)}, u32[]{:S(2)}) collective-permute-start(f32[1024,128]{0,1:T(8,128)S(1)} %all_gather.19), channel_id=1, source_target_pairs={{0,16},{4,20},{8,24},{12,28},{16,0},{20,4},{24,8},{28,12},{32,48},... | collective-permute-start | bytes 1572872 | tf_op jit(solution)/shard_map/ppermute | solution.py:12
  199.6 16.8 %collective-permute-done.2 = f32[1024,128]{0,1:T(8,128)S(1)} collective-permute-done((f32[1024,128]{0,1:T(8,128)S(1)}, f32[1024,128]{0,1:T(8,128)S(1)}, u32[]{:S(2)}, u32[]{:S(2)}) %collective-permute-start.2) | collective-permute-done | bytes 524320 | tf_op jit(solution)/shard_map/ppermute | solution.py:12
  221.8 13.3 %all_gather.20 = f32[1024,128]{0,1:T(8,128)S(1)} all-gather(f32[256,128]{0,1:T(8,128)S(1)} %fusion.6), channel_id=1, replica_groups=mesh['sub'=128,'case'=4] {'case'}, dimensions={0}, use_global_device_ids=true | all-gather | bytes 655360 | tf_op jit(solution)/shard_map/all_gather | solution.py:81
  235.1 7.6 %collective-permute-start.3 = (f32[1024,128]{0,1:T(8,128)S(1)}, f32[1024,128]{0,1:T(8,128)S(1)}, u32[]{:S(2)}, u32[]{:S(2)}) collective-permute-start(f32[1024,128]{0,1:T(8,128)S(1)} %all_gather.20), channel_id=1, source_target_pairs={{0,32},{4,36},{8,40},{12,44},{16,48},{20,52},{24,56},{28,60},{32,0... | collective-permute-start | bytes 1572872 | tf_op jit(solution)/shard_map/ppermute | solution.py:12
  242.8 40.0 %collective-permute-done.3 = f32[1024,128]{0,1:T(8,128)S(1)} collective-permute-done((f32[1024,128]{0,1:T(8,128)S(1)}, f32[1024,128]{0,1:T(8,128)S(1)}, u32[]{:S(2)}, u32[]{:S(2)}) %collective-permute-start.3) | collective-permute-done | bytes 524320 | tf_op jit(solution)/shard_map/ppermute | solution.py:12
  288.1 12.8 %all_gather.21 = f32[1024,128]{0,1:T(8,128)S(1)} all-gather(f32[256,128]{0,1:T(8,128)S(1)} %fusion.5), channel_id=1, replica_groups=mesh['sub'=128,'case'=4] {'case'}, dimensions={0}, use_global_device_ids=true | all-gather | bytes 655360 | tf_op jit(solution)/shard_map/all_gather | solution.py:81
  300.9 11.2 %collective-permute-start.4 = (f32[1024,128]{0,1:T(8,128)S(1)}, f32[1024,128]{0,1:T(8,128)S(1)}, u32[]{:S(2)}, u32[]{:S(2)}) collective-permute-start(f32[1024,128]{0,1:T(8,128)S(1)} %all_gather.21), channel_id=1, source_target_pairs={{0,64},{4,68},{8,72},{12,76},{16,80},{20,84},{24,88},{28,92},{32,9... | collective-permute-start | bytes 1572872 | tf_op jit(solution)/shard_map/ppermute | solution.py:12
  312.1 36.2 %collective-permute-done.4 = f32[1024,128]{0,1:T(8,128)S(1)} collective-permute-done((f32[1024,128]{0,1:T(8,128)S(1)}, f32[1024,128]{0,1:T(8,128)S(1)}, u32[]{:S(2)}, u32[]{:S(2)}) %collective-permute-start.4) | collective-permute-done | bytes 524320 | tf_op jit(solution)/shard_map/ppermute | solution.py:12
  353.6 13.2 %all_gather.22 = f32[1024,128]{0,1:T(8,128)S(1)} all-gather(f32[256,128]{0,1:T(8,128)S(1)} %fusion.4), channel_id=1, replica_groups=mesh['sub'=128,'case'=4] {'case'}, dimensions={0}, use_global_device_ids=true | all-gather | bytes 655360 | tf_op jit(solution)/shard_map/all_gather | solution.py:81
  366.8 2.4 collective-permute-start.5
  369.3 10.0 %collective-permute-done.5 = f32[1024,128]{0,1:T(8,128)S(1)} collective-permute-done((f32[1024,128]{0,1:T(8,128)S(1)}, f32[1024,128]{0,1:T(8,128)S(1)}, u32[]{:S(2)}, u32[]{:S(2)}) %collective-permute-start.5) | collective-permute-done | bytes 524320 | tf_op jit(solution)/shard_map/ppermute | solution.py:12
  384.6 13.3 %all_gather.23 = f32[1024,128]{0,1:T(8,128)S(1)} all-gather(f32[256,128]{0,1:T(8,128)S(1)} %fusion.3), channel_id=1, replica_groups=mesh['sub'=128,'case'=4] {'case'}, dimensions={0}, use_global_device_ids=true | all-gather | bytes 655360 | tf_op jit(solution)/shard_map/all_gather | solution.py:81
  397.8 4.0 collective-permute-start.6
  403.5 6.9 %collective-permute-done.6 = f32[1024,128]{0,1:T(8,128)S(1)} collective-permute-done((f32[1024,128]{0,1:T(8,128)S(1)}, f32[1024,128]{0,1:T(8,128)S(1)}, u32[]{:S(2)}, u32[]{:S(2)}) %collective-permute-start.6) | collective-permute-done | bytes 524320 | tf_op jit(solution)/shard_map/ppermute | solution.py:12
  (140 shorter events, 53.6 us)
Async XLA Ops:
  7.2 47.8 %copy-start.1 = (s32[1,32]{1,0:T(1,128)S(1)}, s32[1,32]{1,0:T(1,128)}, u32[]{:S(2)}) copy-start(s32[1,32]{1,0:T(1,128)} %param.15) | copy-start | bytes 388
  8.9 36.8 %all-to-all-start = ((f32[1,128,256]{2,0,1:T(1,128)}), f32[1,128,256]{2,0,1:T(1,128)S(1)}, u32[]{:S(2)}, u32[]{:S(2)}) async-start(f32[1,128,256]{2,0,1:T(1,128)} %copy.64), calls=%async_computation | async-start | bytes 262144 | tf_op jit(solution)/shard_map/all_to_all | solution.py:20
  45.7 40.8 %all-to-all-start.1 = ((f32[1,128,1024]{2,0,1:T(1,128)}), f32[1,128,1024]{2,0,1:T(1,128)S(1)}, u32[]{:S(2)}, u32[]{:S(2)}) async-start(f32[1,128,1024]{2,0,1:T(1,128)} %copy.66), calls=%async_computation.1 | async-start | bytes 1048576 | tf_op jit(solution)/shard_map/all_to_all | solution.py:19
  52.9 87.9 %all-reduce.2.cloned.1.call-start = ((), (), s32[]{:S(2)}) async-start(), calls=%async_computation.2 | async-start | bytes 1048576 | tf_op jit(solution)/shard_map/psum | solution.py:52
  54.9 33.8 %copy-start = (s32[1,32]{1,0:T(1,128)S(1)}, s32[1,32]{1,0:T(1,128)}, u32[]{:S(2)}) copy-start(s32[1,32]{1,0:T(1,128)} %param.14) | copy-start | bytes 388
  140.8 4.0 collective-permute-start
  163.6 13.0 %collective-permute-start.1 = (f32[1024,128]{0,1:T(8,128)S(1)}, f32[1024,128]{0,1:T(8,128)S(1)}, u32[]{:S(2)}, u32[]{:S(2)}) collective-permute-start(f32[1024,128]{0,1:T(8,128)S(1)} %all_gather.18), channel_id=1, source_target_pairs={{0,8},{4,12},{8,0},{12,4},{16,24},{20,28},{24,16},{28,20},{32,40},... | collective-permute-start | bytes 1572872 | tf_op jit(solution)/shard_map/ppermute | solution.py:12
  195.1 21.3 %collective-permute-start.2 = (f32[1024,128]{0,1:T(8,128)S(1)}, f32[1024,128]{0,1:T(8,128)S(1)}, u32[]{:S(2)}, u32[]{:S(2)}) collective-permute-start(f32[1024,128]{0,1:T(8,128)S(1)} %all_gather.19), channel_id=1, source_target_pairs={{0,16},{4,20},{8,24},{12,28},{16,0},{20,4},{24,8},{28,12},{32,48},... | collective-permute-start | bytes 1572872 | tf_op jit(solution)/shard_map/ppermute | solution.py:12
  235.1 47.6 %collective-permute-start.3 = (f32[1024,128]{0,1:T(8,128)S(1)}, f32[1024,128]{0,1:T(8,128)S(1)}, u32[]{:S(2)}, u32[]{:S(2)}) collective-permute-start(f32[1024,128]{0,1:T(8,128)S(1)} %all_gather.20), channel_id=1, source_target_pairs={{0,32},{4,36},{8,40},{12,44},{16,48},{20,52},{24,56},{28,60},{32,0... | collective-permute-start | bytes 1572872 | tf_op jit(solution)/shard_map/ppermute | solution.py:12
  300.9 47.4 %collective-permute-start.4 = (f32[1024,128]{0,1:T(8,128)S(1)}, f32[1024,128]{0,1:T(8,128)S(1)}, u32[]{:S(2)}, u32[]{:S(2)}) collective-permute-start(f32[1024,128]{0,1:T(8,128)S(1)} %all_gather.21), channel_id=1, source_target_pairs={{0,64},{4,68},{8,72},{12,76},{16,80},{20,84},{24,88},{28,92},{32,9... | collective-permute-start | bytes 1572872 | tf_op jit(solution)/shard_map/ppermute | solution.py:12
  366.8 12.5 %collective-permute-start.5 = (f32[1024,128]{0,1:T(8,128)S(1)}, f32[1024,128]{0,1:T(8,128)S(1)}, u32[]{:S(2)}, u32[]{:S(2)}) collective-permute-start(f32[1024,128]{0,1:T(8,128)S(1)} %all_gather.22), channel_id=1, source_target_pairs={{0,128},{4,132},{8,136},{12,140},{16,144},{20,148},{24,152},{28,15... | collective-permute-start | bytes 1572872 | tf_op jit(solution)/shard_map/ppermute | solution.py:12
  397.8 12.6 %collective-permute-start.6 = (f32[1024,128]{0,1:T(8,128)S(1)}, f32[1024,128]{0,1:T(8,128)S(1)}, u32[]{:S(2)}, u32[]{:S(2)}) collective-permute-start(f32[1024,128]{0,1:T(8,128)S(1)} %all_gather.23), channel_id=1, source_target_pairs={{0,256},{4,260},{8,264},{12,268},{16,272},{20,276},{24,280},{28,28... | collective-permute-start | bytes 1572872 | tf_op jit(solution)/shard_map/ppermute | solution.py:12
Sparse Core Ops, SparseCore 0:
  91.0 49.8 all-reduce.1
where the time goes:
time: 424 us; the launch traced here: 423 us
  waiting for transfers between devices  215 us (51%)
  blocking collectives  78.5 us (19%)
  starting transfers between devices  62.1 us (15%)
  local copies, waits for them, and re-layouts  32.1 us (8%)
  matrix products  15.4 us (4%)
  between operations  15.3 us (4%)
  other arithmetic  4.42 us (1%)
    ppermute x7, waiting for transfers between devices, from_partner(): return lax.ppermute(value, axis, pairs)  121 us
    all_gather x6, blocking collectives, on_device(): current = lax.all_gather(parent, 'case', axis=0, tiled=True)  78.5 us
    psum x1, waiting for transfers between devices, on_device(): current = lax.psum(contribution, 'case')  50 us
    ppermute x7, starting transfers between devices, from_partner(): return lax.ppermute(value, axis, pairs)  35.3 us
    all_to_all x1, waiting for transfers between devices, on_device(): lax.all_to_all(load_interior, 'sub', split_axis=1, concat_axis=0, tiled=T...  31.4 us
    all_to_all x1, starting transfers between devices, on_device(): lax.all_to_all(load_boundary, 'sub', split_axis=1, concat_axis=0, tiled=T...  19.6 us
    dot_general x7, matrix products, on_device(): jnp.dot(matrix, shared, precision=lax.Precision.HIGHEST)  13.2 us
    all_to_all x1, waiting for transfers between devices, on_device(): lax.all_to_all(load_boundary, 'sub', split_axis=1, concat_axis=0, tiled=T...  12.9 us
  transfers between devices with their start and end apart: 10, of which 10 were waited for; matrix products, arithmetic and copies ran while one was open for 2% of the time, Pallas kernels for 0%

commit v1 on v0

--- a/solution.py
+++ b/solution.py
@@ -4,6 +4,22 @@
 from jax.sharding import PartitionSpec as P
 
 BLK = 64
+
+
+def collect(x, axis, dim):
+    ways, here, step = (lax.axis_size(axis), lax.axis_index(axis), x.shape[dim])
+    shape = [n * ways if d == dim else n for d, n in enumerate(x.shape)]
+    full = lax.dynamic_update_slice_in_dim(jnp.zeros(shape, x.dtype), x, here * step, axis=dim)
+    going_up = going_down = x
+    for far in range(1, ways // 2 + 1):
+        going_up = lax.ppermute(going_up, axis, [(d, (d + 1) % ways) for d in range(ways)])
+        full = lax.dynamic_update_slice_in_dim(full, going_up, (here - far) % ways * step, axis=dim)
+        if 2 * far < ways:
+            going_down = lax.ppermute(going_down, axis, [(d, (d - 1) % ways) for d in range(ways)])
+            full = lax.dynamic_update_slice_in_dim(
+                full, going_down, (here + far) % ways * step, axis=dim
+            )
+    return full
 
 
 def from_partner(value, axis, distance):
@@ -78,7 +94,7 @@
             is_node = jnp.logical_or(is_node, slot == 0)
         nodes = jnp.where(is_node, parent, nodes)
         if level < levels:
-            current = lax.all_gather(parent, "case", axis=0, tiled=True)
+            current = collect(parent, "case", 0)
     return (leaf_share[None], nodes[None])
 
 

time: 424 us -> 449 us (1.059)
  blocking collectives: 78.5 us -> 0 us
  starting transfers between devices: 62.1 us -> 116 us
  waiting for transfers between devices: 215 us -> 263 us
    all_gather x6 -> x0, blocking collectives: 78.5 us -> none  [on_device(): current = lax.all_gather(parent, 'case', axis=0, tiled=True)]
    ppermute x0 -> x18, starting transfers between devices: none -> 53.8 us  [the longest x6 30.3 us: collect(): lax.ppermute(going_down, axis, [(d, (d - 1) % ways) for d in range(ways)])]
    ppermute x0 -> x18, waiting for transfers between devices: none -> 42.1 us  [the longest x12 42 us: collect(): lax.ppermute(going_up, axis, [(d, (d + 1) % ways) for d in range(ways)])]
    ppermute x7, waiting for transfers between devices: 121 us -> 126 us  [from_partner(): return lax.ppermute(value, axis, pairs)]
  transfers between devices with their start and end apart: 10 -> 28, of which waited for: 10 -> 22; matrix products, arithmetic and copies ran while one was open for 2% -> 2% of each run, Pallas kernels for 0% -> 0%
where the time goes in v1:
time: 449 us; the launch traced here: 447 us
  waiting for transfers between devices  263 us (59%)
  starting transfers between devices  116 us (26%)
  local copies, waits for them, and re-layouts  32.9 us (7%)
  between operations  15.8 us (4%)
  matrix products  15.4 us (3%)
    ppermute x7, waiting for transfers between devices, from_partner(): return lax.ppermute(value, axis, pairs)  126 us
    psum x1, waiting for transfers between devices, on_device(): current = lax.psum(contribution, 'case')  49.9 us
    ppermute x12, waiting for transfers between devices, collect(): lax.ppermute(going_up, axis, [(d, (d + 1) % ways) for d in range(ways)])  42 us
    ppermute x7, starting transfers between devices, from_partner(): return lax.ppermute(value, axis, pairs)  35.5 us
    all_to_all x1, waiting for transfers between devices, on_device(): lax.all_to_all(load_interior, 'sub', split_axis=1, concat_axis=0, tiled=T...  31.7 us
    ppermute x6, starting transfers between devices, collect(): lax.ppermute(going_down, axis, [(d, (d - 1) % ways) for d in range(ways)])  30.3 us
    ppermute x12, starting transfers between devices, collect(): lax.ppermute(going_up, axis, [(d, (d + 1) % ways) for d in range(ways)])  23.6 us
    all_to_all x1, starting transfers between devices, on_device(): lax.all_to_all(load_boundary, 'sub', split_axis=1, concat_axis=0, tiled=T...  19.6 us
  transfers between devices with their start and end apart: 28, of which 22 were waited for; matrix products, arithmetic and copies ran while one was open for 2% of the time, Pallas kernels for 0%

profile of v1, /device:TPU:8, one launch (start us, length us, event | category | flops | bytes accessed | tf_op | source)
XLA Modules:
  0.0 447.5 jit_solution(1475301032841218831)
XLA Ops:
  8.9 19.6 %all-to-all-start = ((f32[1,128,256]{2,0,1:T(1,128)}), f32[1,128,256]{2,0,1:T(1,128)S(1)}, u32[]{:S(2)}, u32[]{:S(2)}) async-start(f32[1,128,256]{2,0,1:T(1,128)} %copy.76), calls=%async_computation | async-start | bytes 262144 | tf_op jit(solution)/shard_map/all_to_all | solution.py:36
  32.6 13.1 %all-to-all-done = f32[1,128,256]{2,0,1:T(1,128)S(1)} async-done(((f32[1,128,256]{2,0,1:T(1,128)}), f32[1,128,256]{2,0,1:T(1,128)S(1)}, u32[]{:S(2)}, u32[]{:S(2)}) %all-to-all-start) | async-done | bytes 131104 | tf_op jit(solution)/shard_map/all_to_all | solution.py:36
  45.7 7.2 %all-to-all-start.1 = ((f32[1,128,1024]{2,0,1:T(1,128)}), f32[1,128,1024]{2,0,1:T(1,128)S(1)}, u32[]{:S(2)}, u32[]{:S(2)}) async-start(f32[1,128,1024]{2,0,1:T(1,128)} %copy.78), calls=%async_computation.1 | async-start | bytes 1048576 | tf_op jit(solution)/shard_map/all_to_all | solution.py:35
  54.9 31.7 %all-to-all-done.1 = f32[1,128,1024]{2,0,1:T(1,128)S(1)} async-done(((f32[1,128,1024]{2,0,1:T(1,128)}), f32[1,128,1024]{2,0,1:T(1,128)S(1)}, u32[]{:S(2)}, u32[]{:S(2)}) %all-to-all-start.1) | async-done | bytes 524320 | tf_op jit(solution)/shard_map/all_to_all | solution.py:35
  91.0 49.9 %all-reduce.2.cloned.1.call-done = f32[1024,128]{1,0:T(8,128)} async-done(((f32[1024,128]{1,0:T(8,128)}), f32[1024,128]{1,0:T(8,128)}) %all-reduce.2.cloned.1.call-update) | async-done | bytes 524304 | tf_op jit(solution)/shard_map/psum | solution.py:68
  161.7 6.0 %collective-permute-done.3 = f32[256,128]{0,1:T(8,128)S(1)} collective-permute-done((f32[256,128]{0,1:T(8,128)S(1)}, f32[256,128]{0,1:T(8,128)S(1)}, u32[]{:S(2)}, u32[]{:S(2)}) %collective-permute-start.3) | collective-permute-done | bytes 131104 | tf_op jit(solution)/shard_map/ppermute | solution.py:15
  171.5 10.2 %collective-permute-done.4 = f32[1024,128]{1,0:T(8,128)S(1)} collective-permute-done((f32[1024,128]{1,0:T(8,128)S(1)}, f32[1024,128]{1,0:T(8,128)S(1)}, u32[]{:S(2)}, u32[]{:S(2)}) %collective-permute-start.4) | collective-permute-done | bytes 524320 | tf_op jit(solution)/shard_map/ppermute | solution.py:28
  188.7 5.1 %collective-permute-start.6 = (f32[256,128]{0,1:T(8,128)S(1)}, f32[256,128]{0,1:T(8,128)S(1)}, u32[]{:S(2)}, u32[]{:S(2)}) collective-permute-start(f32[256,128]{0,1:T(8,128)S(1)} %fusion.7), channel_id=1, source_target_pairs={{0,3},{1,0},{2,1},{3,2},{4,7},{5,4},{6,5},{7,6},{8,11},{9,8},{10,9... | collective-permute-start | bytes 393224 | tf_op jit(solution)/shard_map/ppermute | solution.py:18
  196.9 6.0 %collective-permute-done.7 = f32[256,128]{0,1:T(8,128)S(1)} collective-permute-done((f32[256,128]{0,1:T(8,128)S(1)}, f32[256,128]{0,1:T(8,128)S(1)}, u32[]{:S(2)}, u32[]{:S(2)}) %collective-permute-start.7) | collective-permute-done | bytes 131104 | tf_op jit(solution)/shard_map/ppermute | solution.py:15
  207.6 18.2 %collective-permute-done.8 = f32[1024,128]{1,0:T(8,128)S(1)} collective-permute-done((f32[1024,128]{1,0:T(8,128)S(1)}, f32[1024,128]{1,0:T(8,128)S(1)}, u32[]{:S(2)}, u32[]{:S(2)}) %collective-permute-start.8) | collective-permute-done | bytes 524320 | tf_op jit(solution)/shard_map/ppermute | solution.py:28
  232.8 5.1 %collective-permute-start.10 = (f32[256,128]{0,1:T(8,128)S(1)}, f32[256,128]{0,1:T(8,128)S(1)}, u32[]{:S(2)}, u32[]{:S(2)}) collective-permute-start(f32[256,128]{0,1:T(8,128)S(1)} %fusion.6), channel_id=1, source_target_pairs={{0,3},{1,0},{2,1},{3,2},{4,7},{5,4},{6,5},{7,6},{8,11},{9,8},{10,9... | collective-permute-start | bytes 393224 | tf_op jit(solution)/shard_map/ppermute | solution.py:18
  241.0 6.0 %collective-permute-done.11 = f32[256,128]{0,1:T(8,128)S(1)} collective-permute-done((f32[256,128]{0,1:T(8,128)S(1)}, f32[256,128]{0,1:T(8,128)S(1)}, u32[]{:S(2)}, u32[]{:S(2)}) %collective-permute-start.11) | collective-permute-done | bytes 131104 | tf_op jit(solution)/shard_map/ppermute | solution.py:15
  247.1 7.7 %collective-permute-start.12 = (f32[1024,128]{1,0:T(8,128)S(1)}, f32[1024,128]{1,0:T(8,128)S(1)}, u32[]{:S(2)}, u32[]{:S(2)}) collective-permute-start(f32[1024,128]{1,0:T(8,128)S(1)} %constant_dynamic-update-slice_fusion.12), channel_id=1, source_target_pairs={{0,32},{4,36},{8,40},{12,44},{16,48},{20,52},{24,56},{28,60},{32,0... | collective-permute-start | bytes 1572872 | tf_op jit(solution)/shard_map/ppermute | solution.py:28
  254.9 41.3 %collective-permute-done.12 = f32[1024,128]{1,0:T(8,128)S(1)} collective-permute-done((f32[1024,128]{1,0:T(8,128)S(1)}, f32[1024,128]{1,0:T(8,128)S(1)}, u32[]{:S(2)}, u32[]{:S(2)}) %collective-permute-start.12) | collective-permute-done | bytes 524320 | tf_op jit(solution)/shard_map/ppermute | solution.py:28
  303.2 5.1 %collective-permute-start.14 = (f32[256,128]{0,1:T(8,128)S(1)}, f32[256,128]{0,1:T(8,128)S(1)}, u32[]{:S(2)}, u32[]{:S(2)}) collective-permute-start(f32[256,128]{0,1:T(8,128)S(1)} %fusion.5), channel_id=1, source_target_pairs={{0,3},{1,0},{2,1},{3,2},{4,7},{5,4},{6,5},{7,6},{8,11},{9,8},{10,9... | collective-permute-start | bytes 393224 | tf_op jit(solution)/shard_map/ppermute | solution.py:18
  311.9 6.0 %collective-permute-done.15 = f32[256,128]{0,1:T(8,128)S(1)} collective-permute-done((f32[256,128]{0,1:T(8,128)S(1)}, f32[256,128]{0,1:T(8,128)S(1)}, u32[]{:S(2)}, u32[]{:S(2)}) %collective-permute-start.15) | collective-permute-done | bytes 131104 | tf_op jit(solution)/shard_map/ppermute | solution.py:15
  318.0 11.3 %collective-permute-start.16 = (f32[1024,128]{1,0:T(8,128)S(1)}, f32[1024,128]{1,0:T(8,128)S(1)}, u32[]{:S(2)}, u32[]{:S(2)}) collective-permute-start(f32[1024,128]{1,0:T(8,128)S(1)} %constant_dynamic-update-slice_fusion.8), channel_id=1, source_target_pairs={{0,64},{4,68},{8,72},{12,76},{16,80},{20,84},{24,88},{28,92},{32,9... | collective-permute-start | bytes 1572872 | tf_op jit(solution)/shard_map/ppermute | solution.py:28
  329.4 36.1 %collective-permute-done.16 = f32[1024,128]{1,0:T(8,128)S(1)} collective-permute-done((f32[1024,128]{1,0:T(8,128)S(1)}, f32[1024,128]{1,0:T(8,128)S(1)}, u32[]{:S(2)}, u32[]{:S(2)}) %collective-permute-start.16) | collective-permute-done | bytes 524320 | tf_op jit(solution)/shard_map/ppermute | solution.py:28
  372.5 5.1 %collective-permute-start.18 = (f32[256,128]{0,1:T(8,128)S(1)}, f32[256,128]{0,1:T(8,128)S(1)}, u32[]{:S(2)}, u32[]{:S(2)}) collective-permute-start(f32[256,128]{0,1:T(8,128)S(1)} %fusion.4), channel_id=1, source_target_pairs={{0,3},{1,0},{2,1},{3,2},{4,7},{5,4},{6,5},{7,6},{8,11},{9,8},{10,9... | collective-permute-start | bytes 393224 | tf_op jit(solution)/shard_map/ppermute | solution.py:18
  381.1 6.0 %collective-permute-done.19 = f32[256,128]{0,1:T(8,128)S(1)} collective-permute-done((f32[256,128]{0,1:T(8,128)S(1)}, f32[256,128]{0,1:T(8,128)S(1)}, u32[]{:S(2)}, u32[]{:S(2)}) %collective-permute-start.19) | collective-permute-done | bytes 131104 | tf_op jit(solution)/shard_map/ppermute | solution.py:15
  389.8 11.2 %collective-permute-done.20 = f32[1024,128]{1,0:T(8,128)S(1)} collective-permute-done((f32[1024,128]{1,0:T(8,128)S(1)}, f32[1024,128]{1,0:T(8,128)S(1)}, u32[]{:S(2)}, u32[]{:S(2)}) %collective-permute-start.20) | collective-permute-done | bytes 524320 | tf_op jit(solution)/shard_map/ppermute | solution.py:28
  408.1 5.1 %collective-permute-start.22 = (f32[256,128]{0,1:T(8,128)S(1)}, f32[256,128]{0,1:T(8,128)S(1)}, u32[]{:S(2)}, u32[]{:S(2)}) collective-permute-start(f32[256,128]{0,1:T(8,128)S(1)} %fusion.3), channel_id=1, source_target_pairs={{0,3},{1,0},{2,1},{3,2},{4,7},{5,4},{6,5},{7,6},{8,11},{9,8},{10,9... | collective-permute-start | bytes 393224 | tf_op jit(solution)/shard_map/ppermute | solution.py:18
  416.2 6.0 %collective-permute-done.23 = f32[256,128]{0,1:T(8,128)S(1)} collective-permute-done((f32[256,128]{0,1:T(8,128)S(1)}, f32[256,128]{0,1:T(8,128)S(1)}, u32[]{:S(2)}, u32[]{:S(2)}) %collective-permute-start.23) | collective-permute-done | bytes 131104 | tf_op jit(solution)/shard_map/ppermute | solution.py:15
  427.9 7.0 %collective-permute-done.24 = f32[1024,128]{1,0:T(8,128)S(1)} collective-permute-done((f32[1024,128]{1,0:T(8,128)S(1)}, f32[1024,128]{1,0:T(8,128)S(1)}, u32[]{:S(2)}, u32[]{:S(2)}) %collective-permute-start.24) | collective-permute-done | bytes 524320 | tf_op jit(solution)/shard_map/ppermute | solution.py:28
  (211 shorter events, 105.6 us)
Async XLA Ops:
  8.9 36.8 %all-to-all-start = ((f32[1,128,256]{2,0,1:T(1,128)}), f32[1,128,256]{2,0,1:T(1,128)S(1)}, u32[]{:S(2)}, u32[]{:S(2)}) async-start(f32[1,128,256]{2,0,1:T(1,128)} %copy.76), calls=%async_computation | async-start | bytes 262144 | tf_op jit(solution)/shard_map/all_to_all | solution.py:36
  45.7 40.9 %all-to-all-start.1 = ((f32[1,128,1024]{2,0,1:T(1,128)}), f32[1,128,1024]{2,0,1:T(1,128)S(1)}, u32[]{:S(2)}, u32[]{:S(2)}) async-start(f32[1,128,1024]{2,0,1:T(1,128)} %copy.78), calls=%async_computation.1 | async-start | bytes 1048576 | tf_op jit(solution)/shard_map/all_to_all | solution.py:35
  52.9 87.9 %all-reduce.2.cloned.1.call-start = ((), (), s32[]{:S(2)}) async-start(), calls=%async_computation.2 | async-start | bytes 1048576 | tf_op jit(solution)/shard_map/psum | solution.py:68
  150.9 8.6 %collective-permute-start.1 = (f32[256,128]{0,1:T(8,128)S(1)}, f32[256,128]{0,1:T(8,128)S(1)}, u32[]{:S(2)}, u32[]{:S(2)}) collective-permute-start(f32[256,128]{0,1:T(8,128)S(1)} %fusion.8), channel_id=1, source_target_pairs={{0,1},{1,2},{2,3},{3,0},{4,5},{5,6},{6,7},{7,4},{8,9},{9,10},{10,1... | collective-permute-start | bytes 393224 | tf_op jit(solution)/shard_map/ppermute | solution.py:15
  153.5 8.1 %collective-permute-start.2 = (f32[256,128]{0,1:T(8,128)S(1)}, f32[256,128]{0,1:T(8,128)S(1)}, u32[]{:S(2)}, u32[]{:S(2)}) collective-permute-start(f32[256,128]{0,1:T(8,128)S(1)} %fusion.8), channel_id=1, source_target_pairs={{0,3},{1,0},{2,1},{3,2},{4,7},{5,4},{6,5},{7,6},{8,11},{9,8},{10,9... | collective-permute-start | bytes 393224 | tf_op jit(solution)/shard_map/ppermute | solution.py:18
  159.6 8.1 %collective-permute-start.3 = (f32[256,128]{0,1:T(8,128)S(1)}, f32[256,128]{0,1:T(8,128)S(1)}, u32[]{:S(2)}, u32[]{:S(2)}) collective-permute-start(f32[256,128]{0,1:T(8,128)S(1)} %collective-permute-done.1), channel_id=1, source_target_pairs={{0,1},{1,2},{2,3},{3,0},{4,5},{5,6},{6,7},{7,4},{8,9},{9,10},{10,1... | collective-permute-start | bytes 393224 | tf_op jit(solution)/shard_map/ppermute | solution.py:15
  167.8 13.9 %collective-permute-start.4 = (f32[1024,128]{1,0:T(8,128)S(1)}, f32[1024,128]{1,0:T(8,128)S(1)}, u32[]{:S(2)}, u32[]{:S(2)}) collective-permute-start(f32[1024,128]{1,0:T(8,128)S(1)} %constant_dynamic-update-slice_fusion.20), channel_id=1, source_target_pairs={{0,8},{4,12},{8,0},{12,4},{16,24},{20,28},{24,16},{28,20},{32,40},... | collective-permute-start | bytes 1572872 | tf_op jit(solution)/shard_map/ppermute | solution.py:28
  186.6 8.1 %collective-permute-start.5 = (f32[256,128]{0,1:T(8,128)S(1)}, f32[256,128]{0,1:T(8,128)S(1)}, u32[]{:S(2)}, u32[]{:S(2)}) collective-permute-start(f32[256,128]{0,1:T(8,128)S(1)} %fusion.7), channel_id=1, source_target_pairs={{0,1},{1,2},{2,3},{3,0},{4,5},{5,6},{6,7},{7,4},{8,9},{9,10},{10,1... | collective-permute-start | bytes 393224 | tf_op jit(solution)/shard_map/ppermute | solution.py:15
  194.8 8.1 %collective-permute-start.7 = (f32[256,128]{0,1:T(8,128)S(1)}, f32[256,128]{0,1:T(8,128)S(1)}, u32[]{:S(2)}, u32[]{:S(2)}) collective-permute-start(f32[256,128]{0,1:T(8,128)S(1)} %collective-permute-done.5), channel_id=1, source_target_pairs={{0,1},{1,2},{2,3},{3,0},{4,5},{5,6},{6,7},{7,4},{8,9},{9,10},{10,1... | collective-permute-start | bytes 393224 | tf_op jit(solution)/shard_map/ppermute | solution.py:15
  203.0 22.8 %collective-permute-start.8 = (f32[1024,128]{1,0:T(8,128)S(1)}, f32[1024,128]{1,0:T(8,128)S(1)}, u32[]{:S(2)}, u32[]{:S(2)}) collective-permute-start(f32[1024,128]{1,0:T(8,128)S(1)} %constant_dynamic-update-slice_fusion.16), channel_id=1, source_target_pairs={{0,16},{4,20},{8,24},{12,28},{16,0},{20,4},{24,8},{28,12},{32,48},... | collective-permute-start | bytes 1572872 | tf_op jit(solution)/shard_map/ppermute | solution.py:28
  230.7 8.1 %collective-permute-start.9 = (f32[256,128]{0,1:T(8,128)S(1)}, f32[256,128]{0,1:T(8,128)S(1)}, u32[]{:S(2)}, u32[]{:S(2)}) collective-permute-start(f32[256,128]{0,1:T(8,128)S(1)} %fusion.6), channel_id=1, source_target_pairs={{0,1},{1,2},{2,3},{3,0},{4,5},{5,6},{6,7},{7,4},{8,9},{9,10},{10,1... | collective-permute-start | bytes 393224 | tf_op jit(solution)/shard_map/ppermute | solution.py:15
  238.9 8.1 %collective-permute-start.11 = (f32[256,128]{0,1:T(8,128)S(1)}, f32[256,128]{0,1:T(8,128)S(1)}, u32[]{:S(2)}, u32[]{:S(2)}) collective-permute-start(f32[256,128]{0,1:T(8,128)S(1)} %collective-permute-done.9), channel_id=1, source_target_pairs={{0,1},{1,2},{2,3},{3,0},{4,5},{5,6},{6,7},{7,4},{8,9},{9,10},{10,1... | collective-permute-start | bytes 393224 | tf_op jit(solution)/shard_map/ppermute | solution.py:15
  247.1 49.1 %collective-permute-start.12 = (f32[1024,128]{1,0:T(8,128)S(1)}, f32[1024,128]{1,0:T(8,128)S(1)}, u32[]{:S(2)}, u32[]{:S(2)}) collective-permute-start(f32[1024,128]{1,0:T(8,128)S(1)} %constant_dynamic-update-slice_fusion.12), channel_id=1, source_target_pairs={{0,32},{4,36},{8,40},{12,44},{16,48},{20,52},{24,56},{28,60},{32,0... | collective-permute-start | bytes 1572872 | tf_op jit(solution)/shard_map/ppermute | solution.py:28
  301.2 8.5 %collective-permute-start.13 = (f32[256,128]{0,1:T(8,128)S(1)}, f32[256,128]{0,1:T(8,128)S(1)}, u32[]{:S(2)}, u32[]{:S(2)}) collective-permute-start(f32[256,128]{0,1:T(8,128)S(1)} %fusion.5), channel_id=1, source_target_pairs={{0,1},{1,2},{2,3},{3,0},{4,5},{5,6},{6,7},{7,4},{8,9},{9,10},{10,1... | collective-permute-start | bytes 393224 | tf_op jit(solution)/shard_map/ppermute | solution.py:15
  303.2 8.5 %collective-permute-start.14 = (f32[256,128]{0,1:T(8,128)S(1)}, f32[256,128]{0,1:T(8,128)S(1)}, u32[]{:S(2)}, u32[]{:S(2)}) collective-permute-start(f32[256,128]{0,1:T(8,128)S(1)} %fusion.5), channel_id=1, source_target_pairs={{0,3},{1,0},{2,1},{3,2},{4,7},{5,4},{6,5},{7,6},{8,11},{9,8},{10,9... | collective-permute-start | bytes 393224 | tf_op jit(solution)/shard_map/ppermute | solution.py:18
  309.8 8.1 %collective-permute-start.15 = (f32[256,128]{0,1:T(8,128)S(1)}, f32[256,128]{0,1:T(8,128)S(1)}, u32[]{:S(2)}, u32[]{:S(2)}) collective-permute-start(f32[256,128]{0,1:T(8,128)S(1)} %collective-permute-done.13), channel_id=1, source_target_pairs={{0,1},{1,2},{2,3},{3,0},{4,5},{5,6},{6,7},{7,4},{8,9},{9,10},{10,1... | collective-permute-start | bytes 393224 | tf_op jit(solution)/shard_map/ppermute | solution.py:15
  318.0 47.5 %collective-permute-start.16 = (f32[1024,128]{1,0:T(8,128)S(1)}, f32[1024,128]{1,0:T(8,128)S(1)}, u32[]{:S(2)}, u32[]{:S(2)}) collective-permute-start(f32[1024,128]{1,0:T(8,128)S(1)} %constant_dynamic-update-slice_fusion.8), channel_id=1, source_target_pairs={{0,64},{4,68},{8,72},{12,76},{16,80},{20,84},{24,88},{28,92},{32,9... | collective-permute-start | bytes 1572872 | tf_op jit(solution)/shard_map/ppermute | solution.py:28
  370.4 8.5 %collective-permute-start.17 = (f32[256,128]{0,1:T(8,128)S(1)}, f32[256,128]{0,1:T(8,128)S(1)}, u32[]{:S(2)}, u32[]{:S(2)}) collective-permute-start(f32[256,128]{0,1:T(8,128)S(1)} %fusion.4), channel_id=1, source_target_pairs={{0,1},{1,2},{2,3},{3,0},{4,5},{5,6},{6,7},{7,4},{8,9},{9,10},{10,1... | collective-permute-start | bytes 393224 | tf_op jit(solution)/shard_map/ppermute | solution.py:15
  372.5 8.5 %collective-permute-start.18 = (f32[256,128]{0,1:T(8,128)S(1)}, f32[256,128]{0,1:T(8,128)S(1)}, u32[]{:S(2)}, u32[]{:S(2)}) collective-permute-start(f32[256,128]{0,1:T(8,128)S(1)} %fusion.4), channel_id=1, source_target_pairs={{0,3},{1,0},{2,1},{3,2},{4,7},{5,4},{6,5},{7,6},{8,11},{9,8},{10,9... | collective-permute-start | bytes 393224 | tf_op jit(solution)/shard_map/ppermute | solution.py:18
  379.1 8.1 %collective-permute-start.19 = (f32[256,128]{0,1:T(8,128)S(1)}, f32[256,128]{0,1:T(8,128)S(1)}, u32[]{:S(2)}, u32[]{:S(2)}) collective-permute-start(f32[256,128]{0,1:T(8,128)S(1)} %collective-permute-done.17), channel_id=1, source_target_pairs={{0,1},{1,2},{2,3},{3,0},{4,5},{5,6},{6,7},{7,4},{8,9},{9,10},{10,1... | collective-permute-start | bytes 393224 | tf_op jit(solution)/shard_map/ppermute | solution.py:15
  387.3 13.7 %collective-permute-start.20 = (f32[1024,128]{1,0:T(8,128)S(1)}, f32[1024,128]{1,0:T(8,128)S(1)}, u32[]{:S(2)}, u32[]{:S(2)}) collective-permute-start(f32[1024,128]{1,0:T(8,128)S(1)} %constant_dynamic-update-slice_fusion.4), channel_id=1, source_target_pairs={{0,128},{4,132},{8,136},{12,140},{16,144},{20,148},{24,152},{28,15... | collective-permute-start | bytes 1572872 | tf_op jit(solution)/shard_map/ppermute | solution.py:28
  406.0 8.1 %collective-permute-start.21 = (f32[256,128]{0,1:T(8,128)S(1)}, f32[256,128]{0,1:T(8,128)S(1)}, u32[]{:S(2)}, u32[]{:S(2)}) collective-permute-start(f32[256,128]{0,1:T(8,128)S(1)} %fusion.3), channel_id=1, source_target_pairs={{0,1},{1,2},{2,3},{3,0},{4,5},{5,6},{6,7},{7,4},{8,9},{9,10},{10,1... | collective-permute-start | bytes 393224 | tf_op jit(solution)/shard_map/ppermute | solution.py:15
  414.1 8.1 %collective-permute-start.23 = (f32[256,128]{0,1:T(8,128)S(1)}, f32[256,128]{0,1:T(8,128)S(1)}, u32[]{:S(2)}, u32[]{:S(2)}) collective-permute-start(f32[256,128]{0,1:T(8,128)S(1)} %collective-permute-done.21), channel_id=1, source_target_pairs={{0,1},{1,2},{2,3},{3,0},{4,5},{5,6},{6,7},{7,4},{8,9},{9,10},{10,1... | collective-permute-start | bytes 393224 | tf_op jit(solution)/shard_map/ppermute | solution.py:15
  422.3 12.6 %collective-permute-start.24 = (f32[1024,128]{1,0:T(8,128)S(1)}, f32[1024,128]{1,0:T(8,128)S(1)}, u32[]{:S(2)}, u32[]{:S(2)}) collective-permute-start(f32[1024,128]{1,0:T(8,128)S(1)} %constant_dynamic-update-slice_fusion), channel_id=1, source_target_pairs={{0,256},{4,260},{8,264},{12,268},{16,272},{20,276},{24,280},{28,28... | collective-permute-start | bytes 1572872 | tf_op jit(solution)/shard_map/ppermute | solution.py:28
  (6 other events, 109.7 us)
Sparse Core Ops, SparseCore 0:
  91.0 49.8 all-reduce.1
